TPU v7x, 256 devices: a whole 4x4x8 slice. The times are simulated.
256 devices in a mesh: hid: 32 (over z_hi, x, core), wid: 8 (over z_lo, y).
Axes of the slice: x: 4, y: 4, z: 8 (z_hi: 4, z_lo: 2; z = z_hi * 2 + z_lo), core: 2. Of those that a mesh axis runs over, the one named last changes fastest.
Arguments:
- inputs: bfloat16 [768, 8192], P('hid', 'wid'), may hold values from -6 to 6
- gate_weight: bfloat16 [8192, 28672], P('wid', 'hid'), may hold values from -0.0625 to 0.0625
- up_weight: bfloat16 [8192, 28672], P('wid', 'hid'), may hold values from -0.0625 to 0.0625
- down_weight: bfloat16 [28672, 8192], P('hid', 'wid'), may hold values from -0.03125 to 0.03125
- out_grad: bfloat16 [768, 8192], P('hid', 'wid'), may hold values from -0.43164062 to 0.43164062
Outputs:
- input_grad: bfloat16 [768, 8192], P('hid', 'wid')
- gate_grad: bfloat16 [8192, 28672], P('wid', 'hid')
- up_grad: bfloat16 [8192, 28672], P('wid', 'hid')
- down_grad: bfloat16 [28672, 8192], P('hid', 'wid')
All inputs are finite; a program needn't handle non-finite values.
Results may differ from a plain program's by a relative error of at most 0.02.
Values may be sent and summed in bfloat16 or wider, within the bound.
No kernel may reach another device: no remote copies, remote signals or barrier semaphores. Data moves between devices by JAX's collectives and lax.ppermute only.
A program may use at most 64 MiB of HBM per device.

v0:
```python
import jax
import jax.numpy as jnp
from jax import lax
from jax.sharding import Mesh, PartitionSpec as P


def swiglu_terms(gate, up, hidden_grad):
    sigma = jax.nn.sigmoid(gate)
    hidden = (gate * sigma * up).astype(jnp.bfloat16)
    up_term = (hidden_grad * gate * sigma).astype(jnp.bfloat16)
    gate_term = (hidden_grad * up * sigma * (1.0 + gate * (1.0 - sigma))).astype(jnp.bfloat16)
    return (hidden, gate_term, up_term)


def make_per_device(n_hid, n_wid):

    def per_device(inputs, gate_weight, up_weight, down_weight, out_grad):
        dw = inputs.shape[1]
        ff = gate_weight.shape[1]
        both = lax.all_gather(
            jnp.concatenate([inputs, out_grad], 1), ("chip", "core"), axis=0, tiled=True
        )
        all_inputs, all_grads = (both[:, :dw], both[:, dw:])
        tokens = all_inputs.shape[0]
        contract_last = (((1,), (1,)), ((), ()))
        gate_part = jnp.dot(all_inputs, gate_weight, preferred_element_type=jnp.float32)
        up_part = jnp.dot(all_inputs, up_weight, preferred_element_type=jnp.float32)
        grad_part = lax.dot_general(
            all_grads, down_weight, contract_last, preferred_element_type=jnp.float32
        )
        parts = jnp.concatenate([gate_part, up_part, grad_part], 1).astype(jnp.bfloat16)
        parts = lax.all_to_all(
            parts.reshape(n_wid, tokens // n_wid, 3 * ff), "wid", 0, 0, tiled=False
        )
        sums = jnp.sum(parts.astype(jnp.float32), 0)
        gate, up, hidden_grad = (sums[:, :ff], sums[:, ff : 2 * ff], sums[:, 2 * ff :])
        hidden, gate_term, up_term = swiglu_terms(gate, up, hidden_grad)
        hidden = lax.all_gather(hidden, "wid", axis=0, tiled=True)
        terms = jnp.concatenate([gate_term, up_term], 1)
        terms = jnp.broadcast_to(terms[None], (n_wid,) + terms.shape)
        terms = lax.all_to_all(terms, "wid", 0, 0, tiled=False).reshape(tokens, 2 * ff)
        gate_term, up_term = (terms[:, :ff], terms[:, ff:])
        core = lax.axis_index("core")
        by_core = (n_hid // 2, 2, tokens // n_hid, ff)

        def rows_of(which):
            g = lax.dynamic_index_in_dim(gate_term.reshape(by_core), which, 1, keepdims=False)
            u = lax.dynamic_index_in_dim(up_term.reshape(by_core), which, 1, keepdims=False)
            return lax.dot_general(
                g.reshape(-1, ff), gate_weight, contract_last, preferred_element_type=jnp.float32
            ) + lax.dot_general(
                u.reshape(-1, ff), up_weight, contract_last, preferred_element_type=jnp.float32
            )

        sent = lax.ppermute(rows_of(1 - core).astype(jnp.bfloat16), "core", [(0, 1), (1, 0)])
        total = rows_of(core) + sent.astype(jnp.float32)
        total = total.reshape(n_hid // 2, tokens // n_hid, dw)
        total = lax.all_to_all(total.astype(jnp.bfloat16), "chip", 0, 0, tiled=False)
        input_grad = jnp.sum(total.astype(jnp.float32), 0).astype(jnp.bfloat16)
        contract_first = (((0,), (0,)), ((), ()))
        gate_grad = lax.dot_general(
            all_inputs, gate_term, contract_first, preferred_element_type=jnp.float32
        ).astype(jnp.bfloat16)
        up_grad = lax.dot_general(
            all_inputs, up_term, contract_first, preferred_element_type=jnp.float32
        ).astype(jnp.bfloat16)
        down_grad = lax.dot_general(
            hidden, all_grads, contract_first, preferred_element_type=jnp.float32
        ).astype(jnp.bfloat16)
        return (input_grad, gate_grad, up_grad, down_grad)

    return per_device


def solution(mesh):
    n_hid, n_wid = (mesh.shape["hid"], mesh.shape["wid"])
    split = Mesh(mesh.devices.reshape(n_hid // 2, 2, n_wid), ("chip", "core", "wid"))
    hid = ("chip", "core")
    placed = (P(hid, "wid"), P("wid", hid), P("wid", hid), P(hid, "wid"), P(hid, "wid"))
    return jax.shard_map(
        make_per_device(n_hid, n_wid),
        mesh=split,
        in_specs=placed,
        out_specs=(P(hid, "wid"), P("wid", hid), P("wid", hid), P(hid, "wid")),
        check_vma=False,
    )
```

profile of v0, /device:TPU:32, one launch (start us, length us, event | category | flops | bytes accessed | tf_op | source)
XLA Modules:
  0.0 225.8 jit_solution(1284275522411784669)
XLA Ops:
  7.2 0.0 copy-start
  7.2 0.0 all-gather.3.cloned.1.call-start
  7.2 1.6 pad_maximum_fusion.2
  8.8 0.0 all-gather.3.cloned.1.call-update
  8.8 60.5 %all-gather.3.cloned.1.call-done = bf16[768,2048]{1,0:T(8,128)(2,1)} async-done(((bf16[24,2048]{1,0:T(8,128)(2,1)}), bf16[768,2048]{1,0:T(8,128)(2,1)}) %all-gather.3.cloned.1.call-update) | async-done | bytes 3145744 | tf_op jit(solution)/shard_map/all_gather | solution.py:20
  69.3 0.0 copy-start.1
  69.3 0.0 copy-start.3
  69.4 3.9 %convolution_convert_fusion.4 = bf16[768,896]{1,0:T(8,128)(2,1)S(1)} fusion(bf16[1024,896]{1,0:T(8,128)(2,1)} %param.7, bf16[768,2048]{1,0:T(8,128)(2,1)} %all-gather.3.cloned.1.call-done), kind=kOutput, calls=%fused_computation.6 | convolution fusion | flops 1409974272 | bytes 4784128 | tf_op jit(solution)/shard_map/dot_general | solution.py:27
  73.3 0.0 copy-done.1
  73.3 0.0 copy-done.3
  73.3 1.9 convolution_convert_fusion.3
  75.2 0.0 copy-done
  75.2 1.8 convolution_convert_fusion.5
  77.0 0.4 pad_maximum_fusion
  77.3 54.2 %all_to_all.15 = bf16[8,96,2688]{2,1,0:T(8,128)(2,1)S(1)} all-to-all(bf16[8,96,2688]{2,1,0:T(8,128)(2,1)S(1)} %pad_maximum_fusion), channel_id=1, replica_groups=mesh['chip'=16,'core'=2,'wid'=8] {'wid'}, dimensions={0} | all-to-all | bytes 8257536 | tf_op jit(solution)/shard_map/all_to_all | solution.py:32
  131.5 0.5 convert_reduce_fusion
  132.1 0.9 multiply_convert_fusion
  133.0 1.8 broadcast_in_dim.2
  134.7 5.7 %all-to-all-start.1 = ((bf16[8,96,1792]{2,1,0:T(8,128)(2,1)}), bf16[8,96,1792]{2,1,0:T(8,128)(2,1)}, u32[]{:S(2)}, u32[]{:S(2)}) async-start(bf16[8,96,1792]{2,1,0:T(8,128)(2,1)} %broadcast_in_dim.2), calls=%async_computation.1 | async-start | bytes 5505024 | tf_op jit(solution)/shard_map/all_to_all | solution.py:41
  140.5 0.0 all-gather.5.cloned.1.call-start
  140.5 0.7 all-gather.5.cloned.1.call-update
  141.2 37.8 %all-to-all-done.1 = bf16[8,96,1792]{2,1,0:T(8,128)(2,1)} async-done(((bf16[8,96,1792]{2,1,0:T(8,128)(2,1)}), bf16[8,96,1792]{2,1,0:T(8,128)(2,1)}, u32[]{:S(2)}, u32[]{:S(2)}) %all-to-all-start.1) | async-done | bytes 2752544 | tf_op jit(solution)/shard_map/all_to_all | solution.py:41
  179.0 2.0 fusion.8
  181.0 0.3 constant_dynamic-slice_fusion.2
  181.3 0.0 copy-start.4
  181.3 1.0 fusion.10
  182.3 0.5 copy-done.4
  182.8 1.0 add_convert_fusion.1
  183.8 0.1 collective-permute-start
  183.9 1.0 fusion.9
  184.9 1.2 collective-permute-done
  186.2 1.9 add_convert_fusion
  188.1 5.6 %all-to-all-start.2 = ((bf16[16,24,1024]{2,1,0:T(8,128)(2,1)}), bf16[16,24,1024]{2,1,0:T(8,128)(2,1)S(1)}, u32[]{:S(2)}, u32[]{:S(2)}) async-start(bf16[16,24,1024]{2,1,0:T(8,128)(2,1)} %bitcast.10), calls=%async_computation.2 | async-start | bytes 1572864 | tf_op jit(solution)/shard_map/all_to_all | solution.py:58
  193.6 0.0 all-gather.5.cloned.1.call-done
  193.7 0.0 copy-start.2
  193.7 4.8 %convolution_convert_fusion = bf16[896,1024]{1,0:T(8,128)(2,1)} fusion(bf16[768,896]{1,0:T(8,128)(2,1)} %all-gather.5.cloned.1.call-done, bf16[768,2048]{1,0:T(8,128)(2,1)} %all-gather.3.cloned.1.call-done), kind=kOutput, calls=%fused_computation.2 | convolution fusion | flops 1410203648 | bytes 4784128 | tf_op jit(solution)/shard_map/dot_general | solution.py:67
  198.5 0.0 copy-done.2
  198.5 4.4 %convolution_convert_fusion.1 = bf16[1024,896]{1,0:T(8,128)(2,1)} fusion(bf16[768,2048]{1,0:T(8,128)(2,1)S(1)} %copy-done.2, bf16[768,1792]{1,0:T(8,128)(2,1)} %bitcast.3), kind=kOutput, calls=%fused_computation.3 | convolution fusion | flops 1410203648 | bytes 4784128 | tf_op jit(solution)/shard_map/dot_general | solution.py:64
  202.9 4.4 %convolution_convert_fusion.2 = bf16[1024,896]{1,0:T(8,128)(2,1)} fusion(bf16[768,2048]{1,0:T(8,128)(2,1)S(1)} %copy-done.2, bf16[768,1792]{1,0:T(8,128)(2,1)} %bitcast.3), kind=kOutput, calls=%fused_computation.4 | convolution fusion | flops 1410203648 | bytes 4784128 | tf_op jit(solution)/shard_map/dot_general | solution.py:61
  207.4 10.9 %all-to-all-done.2 = bf16[16,24,1024]{2,1,0:T(8,128)(2,1)S(1)} async-done(((bf16[16,24,1024]{2,1,0:T(8,128)(2,1)}), bf16[16,24,1024]{2,1,0:T(8,128)(2,1)S(1)}, u32[]{:S(2)}, u32[]{:S(2)}) %all-to-all-start.2) | async-done | bytes 786464 | tf_op jit(solution)/shard_map/all_to_all | solution.py:58
  218.2 0.7 reduce_sum.22
  (1 shorter events, 0.0 us)
Async XLA Ops:
  7.2 68.0 %copy-start = (bf16[1024,896]{1,0:T(8,128)(2,1)S(1)}, bf16[1024,896]{1,0:T(8,128)(2,1)}, u32[]{:S(2)}) copy-start(bf16[1024,896]{1,0:T(8,128)(2,1)} %param.6) | copy-start | bytes 5505028
  7.2 62.2 %all-gather.3.cloned.1.call-start = ((), (), s32[]{:S(2)}) async-start(), calls=%async_computation.3 | async-start | bytes 3244032 | tf_op jit(solution)/shard_map/all_gather | solution.py:20
  69.3 3.9 %copy-start.1 = (bf16[768,2048]{1,0:T(8,128)(2,1)S(1)}, bf16[768,2048]{1,0:T(8,128)(2,1)}, u32[]{:S(2)}) copy-start(bf16[768,2048]{1,0:T(8,128)(2,1)} %all-gather.3.cloned.1.call-done) | copy-start | bytes 9437188
  69.3 3.9 %copy-start.3 = (bf16[896,1024]{1,0:T(8,128)(2,1)S(1)}, bf16[896,1024]{1,0:T(8,128)(2,1)}, u32[]{:S(2)}) copy-start(bf16[896,1024]{1,0:T(8,128)(2,1)} %param.8) | copy-start | bytes 5505028
  134.7 44.3 %all-to-all-start.1 = ((bf16[8,96,1792]{2,1,0:T(8,128)(2,1)}), bf16[8,96,1792]{2,1,0:T(8,128)(2,1)}, u32[]{:S(2)}, u32[]{:S(2)}) async-start(bf16[8,96,1792]{2,1,0:T(8,128)(2,1)} %broadcast_in_dim.2), calls=%async_computation.1 | async-start | bytes 5505024 | tf_op jit(solution)/shard_map/all_to_all | solution.py:41
  140.5 53.2 %all-gather.5.cloned.1.call-start = ((), (), s32[]{:S(2)}) async-start(), calls=%async_computation.4 | async-start | bytes 1548288 | tf_op jit(solution)/shard_map/all_gather | solution.py:38
  181.3 1.5 copy-start.4
  183.8 2.4 %collective-permute-start = (bf16[384,1024]{1,0:T(8,128)(2,1)S(1)}, bf16[384,1024]{1,0:T(8,128)(2,1)S(1)}, u32[]{:S(2)}, u32[]{:S(2)}) collective-permute-start(bf16[384,1024]{1,0:T(8,128)(2,1)S(1)} %add_convert_fusion.1), channel_id=1, source_target_pairs={{0,8},{8,0},{1,9},{9,1},{2,10},{10,2},{3,11},{11,3},{4,12},{12,4},... | collective-permute-start | bytes 2359304 | tf_op jit(solution)/shard_map/ppermute | solution.py:55
  188.1 30.2 %all-to-all-start.2 = ((bf16[16,24,1024]{2,1,0:T(8,128)(2,1)}), bf16[16,24,1024]{2,1,0:T(8,128)(2,1)S(1)}, u32[]{:S(2)}, u32[]{:S(2)}) async-start(bf16[16,24,1024]{2,1,0:T(8,128)(2,1)} %bitcast.10), calls=%async_computation.2 | async-start | bytes 1572864 | tf_op jit(solution)/shard_map/all_to_all | solution.py:58
  193.7 4.8 %copy-start.2 = (bf16[768,2048]{1,0:T(8,128)(2,1)S(1)}, bf16[768,2048]{1,0:T(8,128)(2,1)}, u32[]{:S(2)}) copy-start(bf16[768,2048]{1,0:T(8,128)(2,1)} %all-gather.3.cloned.1.call-done) | copy-start | bytes 9437188
Sparse Core Ops, SparseCore 0:
  11.1 58.1 all-gather.2
  143.7 48.2 all-gather.4
where the time goes:
time: 226 us
  waiting for transfers between devices  111 us (49%)
  blocking collectives  54.2 us (24%)
  matrix products  26.2 us (12%)
  between operations  14.2 us (6%)
  starting transfers between devices  11.4 us (5%)
  local copies, waits for them, and re-layouts  4.54 us (2%)
  other arithmetic  4.13 us (2%)
    all_gather x1, waiting for transfers between devices, per_device(): lax.all_gather(jnp.concatenate([inputs, out_grad], 1), ('chip', 'core'),...  60.5 us
    all_to_all x1, blocking collectives, per_device(): lax.all_to_all(parts.reshape(n_wid, tokens // n_wid, 3 * ff), 'wid', 0, 0...  54.2 us
    all_to_all x1, waiting for transfers between devices, per_device(): lax.all_to_all(terms, 'wid', 0, 0, tiled=False).reshape(tokens, 2 * ff)  37.8 us
    all_to_all x1, waiting for transfers between devices, per_device(): lax.all_to_all(total.astype(jnp.bfloat16), 'chip', 0, 0, tiled=False)  10.9 us
    all_to_all x1, starting transfers between devices, per_device(): lax.all_to_all(terms, 'wid', 0, 0, tiled=False).reshape(tokens, 2 * ff)  5.75 us
    all_to_all x1, starting transfers between devices, per_device(): lax.all_to_all(total.astype(jnp.bfloat16), 'chip', 0, 0, tiled=False)  5.56 us
    dot_general x1, matrix products, per_device(): lax.dot_general(hidden, all_grads, contract_first, preferred_element_type...  4.83 us
  transfers between devices with their start and end apart: 5, of which 4 were waited for; matrix products, arithmetic and copies ran while one was open for 9% of the time, Pallas kernels for 0%

commit v1 on v0

--- a/solution.py
+++ b/solution.py
@@ -17,8 +17,16 @@
     def per_device(inputs, gate_weight, up_weight, down_weight, out_grad):
         dw = inputs.shape[1]
         ff = gate_weight.shape[1]
-        both = lax.all_gather(
-            jnp.concatenate([inputs, out_grad], 1), ("chip", "core"), axis=0, tiled=True
+        both = jnp.concatenate(
+            lax.all_to_all(
+                jnp.stack(
+                    [jnp.concatenate([inputs, out_grad], 1)] * lax.axis_size(("chip", "core"))
+                ),
+                ("chip", "core"),
+                0,
+                0,
+            ),
+            axis=0,
         )
         all_inputs, all_grads = (both[:, :dw], both[:, dw:])
         tokens = all_inputs.shape[0]

time: 226 us -> 247 us (1.093)
  blocking collectives: 54.2 us -> 138 us
  waiting for transfers between devices: 111 us -> 50.6 us
    all_to_all x0 -> x1, blocking collectives: none -> 84.2 us  [per_device(): lax.all_to_all(jnp.stack([jnp.concatenate([inputs, out_grad], 1)] * lax.a...]
    all_gather x1 -> x0, waiting for transfers between devices: 60.5 us -> none  [per_device(): lax.all_gather(jnp.concatenate([inputs, out_grad], 1), ('chip', 'core'),...]
  transfers between devices with their start and end apart: 5 -> 4, of which waited for: 4 -> 3; matrix products, arithmetic and copies ran while one was open for 9% -> 8% of each run, Pallas kernels for 0% -> 0%
where the time goes in v1:
time: 247 us; the launch traced here: 246 us
  blocking collectives  138 us (56%)
  waiting for transfers between devices  50.6 us (20%)
  matrix products  24.1 us (10%)
  between operations  14.2 us (6%)
  starting transfers between devices  10.2 us (4%)
  local copies, waits for them, and re-layouts  5.73 us (2%)
  other arithmetic  3.5 us (1%)
    all_to_all x1, blocking collectives, per_device(): lax.all_to_all(jnp.stack([jnp.concatenate([inputs, out_grad], 1)] * lax.a...  84.2 us
    all_to_all x1, blocking collectives, per_device(): lax.all_to_all(parts.reshape(n_wid, tokens // n_wid, 3 * ff), 'wid', 0, 0...  53.6 us
    all_to_all x1, waiting for transfers between devices, per_device(): lax.all_to_all(terms, 'wid', 0, 0, tiled=False).reshape(tokens, 2 * ff)  37.8 us
    all_to_all x1, waiting for transfers between devices, per_device(): lax.all_to_all(total.astype(jnp.bfloat16), 'chip', 0, 0, tiled=False)  10.8 us
    all_to_all x1, starting transfers between devices, per_device(): lax.all_to_all(terms, 'wid', 0, 0, tiled=False).reshape(tokens, 2 * ff)  5.74 us
  transfers between devices with their start and end apart: 4, of which 3 were waited for; matrix products, arithmetic and copies ran while one was open for 8% of the time, Pallas kernels for 0%

profile of v1, /device:TPU:32, one launch (start us, length us, event | category | flops | bytes accessed | tf_op | source)
XLA Modules:
  0.0 246.1 jit_solution(5362807264249497648)
XLA Ops:
  7.2 0.0 copy-start
  7.2 1.0 pad_maximum_fusion.2
  8.1 0.4 stack.2
  8.5 0.0 copy-start.4
  8.5 84.2 %all_to_all.20 = bf16[32,24,2048]{2,1,0:T(8,128)(2,1)S(1)} all-to-all(bf16[32,24,2048]{2,1,0:T(8,128)(2,1)S(1)} %stack.2), channel_id=1, replica_groups=mesh['chip'=16,'core'=2,'wid'=8] {'chip','core'}, dimensions={0} | all-to-all | bytes 6291456 | tf_op jit(solution)/shard_map/all_to_all | solution.py:21
  92.8 0.0 copy-start.1
  92.8 0.0 copy-done.4
  92.8 0.0 copy-start.3
  92.8 1.8 convolution_convert_fusion.4
  94.6 0.8 copy-done.3
  95.4 1.9 convolution_convert_fusion.3
  97.3 0.0 copy-done.1
  97.3 0.0 copy-done
  97.3 1.8 convolution_convert_fusion.5
  99.1 0.4 pad_maximum_fusion
  99.5 53.6 %all_to_all.21 = bf16[8,96,2688]{2,1,0:T(8,128)(2,1)S(1)} all-to-all(bf16[8,96,2688]{2,1,0:T(8,128)(2,1)S(1)} %pad_maximum_fusion), channel_id=1, replica_groups=mesh['chip'=16,'core'=2,'wid'=8] {'wid'}, dimensions={0} | all-to-all | bytes 8257536 | tf_op jit(solution)/shard_map/all_to_all | solution.py:40
  153.0 0.5 convert_reduce_fusion
  153.6 0.9 multiply_convert_fusion
  154.5 1.8 broadcast_in_dim.2
  156.2 5.7 %all-to-all-start.2 = ((bf16[8,96,1792]{2,1,0:T(8,128)(2,1)}), bf16[8,96,1792]{2,1,0:T(8,128)(2,1)}, u32[]{:S(2)}, u32[]{:S(2)}) async-start(bf16[8,96,1792]{2,1,0:T(8,128)(2,1)} %broadcast_in_dim.2), calls=%async_computation.2 | async-start | bytes 5505024 | tf_op jit(solution)/shard_map/all_to_all | solution.py:49
  162.0 0.0 all-gather.2.cloned.1.call-start
  162.0 0.7 all-gather.2.cloned.1.call-update
  162.7 37.8 %all-to-all-done.2 = bf16[8,96,1792]{2,1,0:T(8,128)(2,1)} async-done(((bf16[8,96,1792]{2,1,0:T(8,128)(2,1)}), bf16[8,96,1792]{2,1,0:T(8,128)(2,1)}, u32[]{:S(2)}, u32[]{:S(2)}) %all-to-all-start.2) | async-done | bytes 2752544 | tf_op jit(solution)/shard_map/all_to_all | solution.py:49
  200.5 2.0 fusion.8
  202.5 0.3 constant_dynamic-slice_fusion.2
  202.8 0.0 copy-start.5
  202.8 1.0 fusion.10
  203.8 0.5 copy-done.5
  204.3 1.0 add_convert_fusion.1
  205.3 0.1 collective-permute-start
  205.4 1.0 fusion.9
  206.4 1.2 collective-permute-done
  207.7 1.9 add_convert_fusion
  209.6 4.4 %all-to-all-start.3 = ((bf16[16,24,1024]{2,1,0:T(8,128)(2,1)}), bf16[16,24,1024]{2,1,0:T(8,128)(2,1)S(1)}, u32[]{:S(2)}, u32[]{:S(2)}) async-start(bf16[16,24,1024]{2,1,0:T(8,128)(2,1)} %bitcast.11), calls=%async_computation.3 | async-start | bytes 1572864 | tf_op jit(solution)/shard_map/all_to_all | solution.py:66
  214.0 0.0 all-gather.2.cloned.1.call-done
  214.0 0.0 copy-start.2
  214.0 4.8 %convolution_convert_fusion = bf16[896,1024]{1,0:T(8,128)(2,1)} fusion(bf16[768,896]{1,0:T(8,128)(2,1)} %all-gather.2.cloned.1.call-done, bf16[768,2048]{1,0:T(8,128)(2,1)} %bitcast.29), kind=kOutput, calls=%fused_computation.2 | convolution fusion | flops 1410203648 | bytes 4784128 | tf_op jit(solution)/shard_map/dot_general | solution.py:75
  218.8 0.0 copy-done.2
  218.8 4.4 %convolution_convert_fusion.1 = bf16[1024,896]{1,0:T(8,128)(2,1)} fusion(bf16[768,2048]{1,0:T(8,128)(2,1)S(1)} %bitcast.30, bf16[768,1792]{1,0:T(8,128)(2,1)} %bitcast.4), kind=kOutput, calls=%fused_computation.3 | convolution fusion | flops 1410203648 | bytes 4784128 | tf_op jit(solution)/shard_map/dot_general | solution.py:72
  223.3 4.4 %convolution_convert_fusion.2 = bf16[1024,896]{1,0:T(8,128)(2,1)} fusion(bf16[768,2048]{1,0:T(8,128)(2,1)S(1)} %bitcast.31, bf16[768,1792]{1,0:T(8,128)(2,1)} %bitcast.4), kind=kOutput, calls=%fused_computation.4 | convolution fusion | flops 1410203648 | bytes 4784128 | tf_op jit(solution)/shard_map/dot_general | solution.py:69
  227.7 10.8 %all-to-all-done.3 = bf16[16,24,1024]{2,1,0:T(8,128)(2,1)S(1)} async-done(((bf16[16,24,1024]{2,1,0:T(8,128)(2,1)}), bf16[16,24,1024]{2,1,0:T(8,128)(2,1)S(1)}, u32[]{:S(2)}, u32[]{:S(2)}) %all-to-all-start.3) | async-done | bytes 786464 | tf_op jit(solution)/shard_map/all_to_all | solution.py:66
  238.5 0.7 reduce_sum.22
  (1 shorter events, 0.0 us)
Async XLA Ops:
  7.2 90.1 %copy-start = (bf16[1024,896]{1,0:T(8,128)(2,1)S(1)}, bf16[1024,896]{1,0:T(8,128)(2,1)}, u32[]{:S(2)}) copy-start(bf16[1024,896]{1,0:T(8,128)(2,1)} %param.6) | copy-start | bytes 5505028
  8.5 84.2 %copy-start.4 = (bf16[1024,896]{1,0:T(8,128)(2,1)S(1)}, bf16[1024,896]{1,0:T(8,128)(2,1)}, u32[]{:S(2)}) copy-start(bf16[1024,896]{1,0:T(8,128)(2,1)} %param.7) | copy-start | bytes 5505028
  92.8 4.5 %copy-start.1 = (bf16[32,24,2048]{2,1,0:T(8,128)(2,1)}, bf16[32,24,2048]{2,1,0:T(8,128)(2,1)S(1)}, u32[]{:S(2)}) copy-start(bf16[32,24,2048]{2,1,0:T(8,128)(2,1)S(1)} %all_to_all.20) | copy-start | bytes 9437188
  92.8 2.6 %copy-start.3 = (bf16[896,1024]{1,0:T(8,128)(2,1)S(1)}, bf16[896,1024]{1,0:T(8,128)(2,1)}, u32[]{:S(2)}) copy-start(bf16[896,1024]{1,0:T(8,128)(2,1)} %param.8) | copy-start | bytes 5505028
  156.2 44.3 %all-to-all-start.2 = ((bf16[8,96,1792]{2,1,0:T(8,128)(2,1)}), bf16[8,96,1792]{2,1,0:T(8,128)(2,1)}, u32[]{:S(2)}, u32[]{:S(2)}) async-start(bf16[8,96,1792]{2,1,0:T(8,128)(2,1)} %broadcast_in_dim.2), calls=%async_computation.2 | async-start | bytes 5505024 | tf_op jit(solution)/shard_map/all_to_all | solution.py:49
  162.0 52.0 %all-gather.2.cloned.1.call-start = ((), (), s32[]{:S(2)}) async-start(), calls=%async_computation.4 | async-start | bytes 1548288 | tf_op jit(solution)/shard_map/all_gather | solution.py:46
  202.8 1.5 copy-start.5
  205.3 2.4 collective-permute-start
  209.6 28.9 %all-to-all-start.3 = ((bf16[16,24,1024]{2,1,0:T(8,128)(2,1)}), bf16[16,24,1024]{2,1,0:T(8,128)(2,1)S(1)}, u32[]{:S(2)}, u32[]{:S(2)}) async-start(bf16[16,24,1024]{2,1,0:T(8,128)(2,1)} %bitcast.11), calls=%async_computation.3 | async-start | bytes 1572864 | tf_op jit(solution)/shard_map/all_to_all | solution.py:66
  214.0 4.8 %copy-start.2 = (bf16[32,24,2048]{2,1,0:T(8,128)(2,1)S(1)}, bf16[32,24,2048]{2,1,0:T(8,128)(2,1)}, u32[]{:S(2)}) copy-start(bf16[32,24,2048]{2,1,0:T(8,128)(2,1)} %copy-done.1) | copy-start | bytes 9437188
Sparse Core Ops, SparseCore 0:
  165.1 48.2 all-gather.1
